TPU v7x, 512 devices: a whole 4x8x8 slice. The times are simulated.
512 devices in a mesh: island: 16 (over z, x_hi), fsdp: 32 (over y, x_lo, core).
Axes of the slice: x: 4 (x_hi: 2, x_lo: 2; x = x_hi * 2 + x_lo), y: 8, z: 8, core: 2. Of those that a mesh axis runs over, the one named last changes fastest.
Arguments:
- block_input: bfloat16 [65536, 8192], P(('island', 'fsdp')), may hold values from -170 to 170
- lang_ids: int32 [65536], P(('island', 'fsdp')), may hold values from 0 to 15
- queries: bfloat16 [65536, 4096], P(('island', 'fsdp')), may hold values from -52 to 52
- saved_keys: bfloat16 [65536, 512], P(('island', 'fsdp')), may hold values from -4 to 4
- out_grad: bfloat16 [65536, 4096], P(('island', 'fsdp')), may hold values from -70 to 70
- local_wv: bfloat16 [16, 8192, 512], P('island', 'fsdp'), may hold values from -8 to 8
- local_gain: bfloat16 [16, 16, 8192], P('island'), may hold values from -3 to 5
- outer_wv: float32 [8192, 512], P('fsdp', 'island'), may hold values from -4 to 4
- wv_momentum: float32 [8192, 512], P('fsdp', 'island'), may hold values from -1.8 to 1.8
- outer_gain: float32 [16, 8192], P('island', 'fsdp'), may hold values from 0.5 to 1.5
- gain_momentum: float32 [16, 8192], P('island', 'fsdp'), may hold values from -1.8 to 1.8
Outputs:
- new_outer_wv: float32 [8192, 512], P('fsdp', 'island')
- new_wv_momentum: float32 [8192, 512], P('fsdp', 'island')
- new_outer_gain: float32 [16, 8192], P('island', 'fsdp')
- new_gain_momentum: float32 [16, 8192], P('island', 'fsdp')
All inputs are finite; a program needn't handle non-finite values.
Results may differ from a plain program's by a relative error of at most 0.00045.
Values may be sent and summed in bfloat16 or wider, within the bound.
No kernel may reach another device: no remote copies, remote signals or barrier semaphores. Data moves between devices by JAX's collectives and lax.ppermute only.
A program may use at most 64 MiB of HBM per device.

v0:
```python
import jax
import jax.numpy as jnp
from jax import lax
from jax.sharding import PartitionSpec as P

HEADS = 32
KV_HEADS = 4
HEAD_DIM = 128
EPSILON = 1e-05
MOMENTUM = 0.9
OUTER_RATE = 0.7
CLIP_SHARE = 0.25


def normalize(input_rows):
    widened = input_rows.astype(jnp.float32)
    average = jnp.mean(widened, axis=-1, keepdims=True)
    centered = widened - average
    variance = jnp.mean(centered * centered, axis=-1, keepdims=True)
    return centered * lax.rsqrt(variance + EPSILON)


def value_grad(query_rows, key_block, grad_rows):
    length = query_rows.shape[0]
    group = HEADS // KV_HEADS
    query_four = query_rows.reshape(length, KV_HEADS, group, HEAD_DIM)
    key_three = key_block.reshape(length, KV_HEADS, HEAD_DIM)
    scores = jnp.einsum(
        "tkgd,skd->kgts", query_four, key_three, preferred_element_type=jnp.float32
    ) * HEAD_DIM ** (-0.5)
    position = jnp.arange(length, dtype=jnp.int32)
    causal = position[:, None] >= position[None, :]
    scores = jnp.where(causal, scores, -jnp.inf)
    row_top = jnp.max(scores, axis=-1, keepdims=True)
    exponent = jnp.exp(scores - row_top)
    weights_bf = (exponent / jnp.sum(exponent, axis=-1, keepdims=True)).astype(jnp.bfloat16)
    grad_four = grad_rows.reshape(length, KV_HEADS, group, HEAD_DIM)
    values = jnp.einsum("kgts,tkgd->skd", weights_bf, grad_four, preferred_element_type=jnp.float32)
    return values.reshape(length, KV_HEADS * HEAD_DIM).astype(jnp.bfloat16)


def body(
    block_input,
    lang_ids,
    queries,
    saved_keys,
    out_grad,
    local_wv,
    local_gain,
    outer_wv,
    wv_momentum,
    outer_gain,
    gain_momentum,
):
    width = block_input.shape[1]
    fsdp_count = lax.axis_size("fsdp")
    island_count = lax.axis_size("island")
    col_block = width // fsdp_count
    kv_width = local_wv.shape[2]
    lang_count = local_gain.shape[1]
    weight_scale = width ** (-0.5)
    col_begin = lax.axis_index("fsdp") * col_block
    standard = normalize(block_input)
    lang_table = lang_ids[None, :] == jnp.arange(lang_count, dtype=jnp.int32)[:, None]
    gain_rows = jnp.dot(
        lang_table.astype(jnp.bfloat16).T, local_gain[0], preferred_element_type=jnp.float32
    )
    normed = (standard * gain_rows).astype(jnp.bfloat16)
    values_grad = value_grad(queries, saved_keys, out_grad)
    weight_rows = local_wv[0]
    col_normed = lax.all_to_all(normed, "fsdp", split_axis=1, concat_axis=0, tiled=True)
    input_grad = (
        jnp.dot(
            values_grad,
            lax.all_gather(weight_rows, "fsdp", axis=0, tiled=True).T,
            preferred_element_type=jnp.float32,
        )
        * weight_scale
    )
    gain_part = jnp.dot(
        lang_table.astype(jnp.float32), standard * input_grad, precision=lax.Precision.HIGHEST
    )
    gain_grad = lax.psum(gain_part, "fsdp")
    wv_grad = (
        jnp.dot(
            col_normed.T,
            lax.all_gather(values_grad, "fsdp", axis=0, tiled=True),
            preferred_element_type=jnp.float32,
        )
        * weight_scale
    )
    wv_square = jnp.sum(wv_grad * wv_grad)
    weight_square = lax.psum(wv_square, "fsdp")
    gain_square = jnp.sum(gain_grad * gain_grad)
    own_grad = lax.dynamic_slice_in_dim(gain_grad, col_begin, col_block, 1)
    wv_clip = jnp.minimum(1.0, CLIP_SHARE * (width * kv_width) ** 0.5 / jnp.sqrt(weight_square))
    gain_clip = jnp.minimum(1.0, CLIP_SHARE * (lang_count * width) ** 0.5 / jnp.sqrt(gain_square))
    new_wv = weight_rows.astype(jnp.float32) - wv_clip * wv_grad
    own_gain = lax.dynamic_slice_in_dim(local_gain[0], col_begin, col_block, 1).astype(jnp.float32)
    new_gain = own_gain - gain_clip * own_grad
    wv_share = kv_width // island_count
    gain_share = lang_count // island_count
    total_wv, total_gain = lax.psum((new_wv, new_gain), "island")
    island_at = lax.axis_index("island")
    total_wv = lax.dynamic_slice_in_dim(total_wv, island_at * wv_share, wv_share, 1)
    total_gain = lax.dynamic_slice_in_dim(total_gain, island_at * gain_share, gain_share, 0)
    delta_wv = outer_wv - total_wv / island_count
    momentum_wv = MOMENTUM * wv_momentum + delta_wv
    result_wv = outer_wv - OUTER_RATE * (delta_wv + MOMENTUM * momentum_wv)
    delta_gain = outer_gain - total_gain / island_count
    momentum_gain = MOMENTUM * gain_momentum + delta_gain
    result_gain = outer_gain - OUTER_RATE * (delta_gain + MOMENTUM * momentum_gain)
    return (result_wv, momentum_wv, result_gain, momentum_gain)


def solution(mesh):
    in_specs = (
        P(("island", "fsdp"), None),
        P(("island", "fsdp")),
        P(("island", "fsdp"), None),
        P(("island", "fsdp"), None),
        P(("island", "fsdp"), None),
        P("island", "fsdp", None),
        P("island", None, None),
        P("fsdp", "island"),
        P("fsdp", "island"),
        P("island", "fsdp"),
        P("island", "fsdp"),
    )
    out_specs = (P("fsdp", "island"), P("fsdp", "island"), P("island", "fsdp"), P("island", "fsdp"))
    return jax.shard_map(body, mesh=mesh, in_specs=in_specs, out_specs=out_specs, check_vma=False)
```

profile of v0, /device:TPU:32, one launch (start us, length us, event | category | flops | bytes accessed | tf_op | source)
XLA Modules:
  0.0 690.6 jit_solution(18145128111917954765)
XLA Ops:
  7.2 0.0 all-gather.4.cloned.1.call-start
  7.2 1.4 copy.48
  8.7 0.9 reshape.40
  9.6 1.6 copy.46
  11.3 2.3 fusion.33
  13.6 2.8 fusion.8
  16.4 0.0 all-gather.6.cloned.1.call-start
  16.5 0.7 all-gather.6.cloned.1.call-update
  17.2 0.4 convert_reduce_fusion
  17.5 0.7 fusion.6
  18.3 0.8 fusion.2
  19.1 1.6 copy.70
  20.7 9.9 %all-to-all-start = ((bf16[128,32,256]{2,0,1:T(8,128)(2,1)}), bf16[128,32,256]{2,0,1:T(8,128)(2,1)}, u32[]{:S(2)}, u32[]{:S(2)}) async-start(bf16[128,32,256]{2,0,1:T(8,128)(2,1)} %bitcast.44), calls=%async_computation | async-start | bytes 4194304 | tf_op jit(solution)/shard_map/all_to_all | solution.py:71
  30.6 0.0 all-reduce.3.cloned.1.call-start
  30.7 0.1 copy.34
  30.8 54.8 %all-to-all-done = bf16[128,32,256]{2,0,1:T(8,128)(2,1)} async-done(((bf16[128,32,256]{2,0,1:T(8,128)(2,1)}), bf16[128,32,256]{2,0,1:T(8,128)(2,1)}, u32[]{:S(2)}, u32[]{:S(2)}) %all-to-all-start) | async-done | bytes 2097184 | tf_op jit(solution)/shard_map/all_to_all | solution.py:71
  85.6 35.3 %all-gather.4.cloned.1.call-done = bf16[4096,512]{0,1:T(8,128)(2,1)} async-done(((bf16[128,512]{0,1:T(8,128)(2,1)}), bf16[4096,512]{0,1:T(8,128)(2,1)}) %all-gather.4.cloned.1.call-update) | async-done | bytes 4194320 | tf_op jit(solution)/shard_map/all_gather | solution.py:87
  120.9 4.8 multiply_reduce_fusion.1
  125.7 55.3 %psum.28 = f32[]{:T(128)} all-reduce(f32[]{:T(128)} %get-tuple-element.18), channel_id=1, replica_groups=mesh['island'=16,'fsdp'=32] {'fsdp'}, use_global_device_ids=true, to_apply=%region_5.6 | all-reduce | flops 1 | bytes 8 | tf_op jit(solution)/shard_map/psum | solution.py:93
  181.0 0.2 copy.40
  181.9 0.9 convert_subtract_fusion.1
  182.8 0.0 all-reduce.5.cloned.1.call-start
  182.9 16.3 %all-gather.6.cloned.1.call-done = bf16[1,8192,512]{2,1,0:T(8,128)(2,1)} async-done(((bf16[1,256,512]{2,1,0:T(8,128)(2,1)}), bf16[1,8192,512]{2,1,0:T(8,128)(2,1)}) %all-gather.6.cloned.1.call-update) | async-done | bytes 8388624 | tf_op jit(solution)/shard_map/all_gather | solution.py:75
  199.2 6.6 fusion.1
  205.8 2.3 fusion.24
  208.1 161.1 %all-reduce.3.cloned.1.call-done = f32[256,512]{0,1:T(8,128)} async-done(((f32[256,512]{0,1:T(8,128)}), f32[256,512]{0,1:T(8,128)}) %all-reduce.3.cloned.1.call-update) | async-done | bytes 524304 | tf_op jit(solution)/shard_map/psum | solution.py:103
  369.2 1.4 multiply_subtract_fusion
  370.6 231.6 %all-reduce.5.cloned.1.call-done = f32[16,8192]{1,0:T(8,128)} async-done(((f32[16,8192]{1,0:T(8,128)}), f32[16,8192]{1,0:T(8,128)}) %all-reduce.5.cloned.1.call-update) | async-done | bytes 524304 | tf_op jit(solution)/shard_map/psum | solution.py:83
  602.2 1.8 multiply_reduce_fusion
  604.7 0.7 convert_subtract_fusion.2
  605.4 78.1 %psum.31 = f32[16,256]{1,0:T(8,128)S(1)} all-reduce(f32[16,256]{1,0:T(8,128)S(1)} %convert_subtract_fusion.2), channel_id=1, replica_groups=mesh['island'=16,'fsdp'=32] {'island'}, use_global_device_ids=true, to_apply=%region_9.10 | all-reduce | flops 4096 | bytes 32768 | tf_op jit(solution)/shard_map/psum | solution.py:103
  683.5 0.6 multiply_subtract_fusion.2
  (24 shorter events, 0.1 us)
Async XLA Ops:
  7.2 113.7 %all-gather.4.cloned.1.call-start = ((), (), s32[]{:S(2)}) async-start(), calls=%async_computation.1 | async-start | bytes 4325376 | tf_op jit(solution)/shard_map/all_gather | solution.py:87
  13.5 3.6 copy-start
  16.4 1.9 copy-start.7
  16.4 1.9 copy-start.8
  16.4 182.7 %all-gather.6.cloned.1.call-start = ((), (), s32[]{:S(2)}) async-start(), calls=%async_computation.4 | async-start | bytes 8650752 | tf_op jit(solution)/shard_map/all_gather | solution.py:75
  19.1 11.6 %copy-start.1 = (bf16[1,256,512]{2,1,0:T(8,128)(2,1)S(1)}, bf16[1,256,512]{2,1,0:T(8,128)(2,1)}, u32[]{:S(2)}) copy-start(bf16[1,256,512]{2,1,0:T(8,128)(2,1)} %param.16) | copy-start | bytes 786436
  20.7 64.9 %all-to-all-start = ((bf16[128,32,256]{2,0,1:T(8,128)(2,1)}), bf16[128,32,256]{2,0,1:T(8,128)(2,1)}, u32[]{:S(2)}, u32[]{:S(2)}) async-start(bf16[128,32,256]{2,0,1:T(8,128)(2,1)} %bitcast.44), calls=%async_computation | async-start | bytes 4194304 | tf_op jit(solution)/shard_map/all_to_all | solution.py:71
  30.6 338.6 %all-reduce.3.cloned.1.call-start = ((), (), s32[]{:S(2)}) async-start(), calls=%async_computation.2 | async-start | bytes 1048576 | tf_op jit(solution)/shard_map/psum | solution.py:103
  120.9 78.3 %copy-start.2 = (bf16[4,128,128]{1,2,0:T(8,128)(2,1)S(1)}, bf16[4,128,128]{1,2,0:T(8,128)(2,1)}, u32[]{:S(2)}) copy-start(bf16[4,128,128]{1,2,0:T(8,128)(2,1)} %fusion.8) | copy-start | bytes 393220
  182.8 419.4 %all-reduce.5.cloned.1.call-start = ((), (), s32[]{:S(2)}) async-start(), calls=%async_computation.3 | async-start | bytes 1048576 | tf_op jit(solution)/shard_map/psum | solution.py:83
  205.7 163.4 %copy-start.3 = (f32[256,32]{0,1:T(8,128)S(1)}, f32[256,32]{0,1:T(8,128)}, u32[]{:S(2)}) copy-start(f32[256,32]{0,1:T(8,128)} %param.18) | copy-start | bytes 98308
  205.8 163.4 %copy-start.4 = (f32[256,32]{0,1:T(8,128)S(1)}, f32[256,32]{0,1:T(8,128)}, u32[]{:S(2)}) copy-start(f32[256,32]{0,1:T(8,128)} %param.19) | copy-start | bytes 98308
  205.8 477.7 %copy-start.5 = (f32[1,256]{1,0:T(1,128)S(1)}, f32[1,256]{1,0:T(1,128)}, u32[]{:S(2)}) copy-start(f32[1,256]{1,0:T(1,128)} %param.20) | copy-start | bytes 3076
  205.8 477.7 %copy-start.6 = (f32[1,256]{1,0:T(1,128)S(1)}, f32[1,256]{1,0:T(1,128)}, u32[]{:S(2)}) copy-start(f32[1,256]{1,0:T(1,128)} %param.21) | copy-start | bytes 3076
Sparse Core Ops, SparseCore 0:
  16.5 104.2 all-gather.3
  123.0 76.1 all-gather.5
  202.1 167.0 all-reduce.2
  371.9 230.2 all-reduce.4
where the time goes:
time: 691 us
  waiting for transfers between devices  500 us (72%)
  blocking collectives  133 us (19%)
  matrix products  19.6 us (3%)
  between operations  15.3 us (2%)
  starting transfers between devices  10.1 us (1%)
    psum x1, waiting for transfers between devices, body(): gain_grad = lax.psum(gain_part, 'fsdp')  232 us
    psum x1, waiting for transfers between devices, body(): total_wv, total_gain = lax.psum((new_wv, new_gain), 'island')  161 us
    psum x1, blocking collectives, body(): total_wv, total_gain = lax.psum((new_wv, new_gain), 'island')  78.1 us
    psum x1, blocking collectives, body(): weight_square = lax.psum(wv_square, 'fsdp')  55.3 us
    all_to_all x1, waiting for transfers between devices, body(): lax.all_to_all(normed, 'fsdp', split_axis=1, concat_axis=0, tiled=True)  54.8 us
    all_gather x1, waiting for transfers between devices, body(): lax.all_gather(values_grad, 'fsdp', axis=0, tiled=True)  35.3 us
    all_gather x1, waiting for transfers between devices, body(): lax.all_gather(weight_rows, 'fsdp', axis=0, tiled=True)  16.3 us
  transfers between devices with their start and end apart: 5, of which 5 were waited for; matrix products, arithmetic and copies ran while one was open for 3% of the time, Pallas kernels for 0%

commit v1 on v0

--- a/solution.py
+++ b/solution.py
@@ -10,6 +10,13 @@
 MOMENTUM = 0.9
 OUTER_RATE = 0.7
 CLIP_SHARE = 0.25
+
+
+def swapped_in(x, name, d):
+    count = lax.axis_size(name)
+    pieces = jnp.stack([x for _ in range(count)])
+    pieces = lax.all_to_all(pieces, name, split_axis=0, concat_axis=0)
+    return jnp.concatenate(pieces, axis=d)
 
 
 def normalize(input_rows):
@@ -83,9 +90,7 @@
     gain_grad = lax.psum(gain_part, "fsdp")
     wv_grad = (
         jnp.dot(
-            col_normed.T,
-            lax.all_gather(values_grad, "fsdp", axis=0, tiled=True),
-            preferred_element_type=jnp.float32,
+            col_normed.T, swapped_in(values_grad, "fsdp", 0), preferred_element_type=jnp.float32
         )
         * weight_scale
     )

time: 691 us -> 764 us (1.11)
  waiting for transfers between devices: 500 us -> 550 us
  starting transfers between devices: 10.1 us -> 19.9 us
    all_to_all x0 -> x1, waiting for transfers between devices: none -> 101 us  [swapped_in(): pieces = lax.all_to_all(pieces, name, split_axis=0, concat_axis=0)]
    all_gather x1 -> x0, waiting for transfers between devices: 35.3 us -> none  [body(): lax.all_gather(values_grad, 'fsdp', axis=0, tiled=True)]
    all_gather x1, waiting for transfers between devices: 16.3 us -> 0.02 us  [body(): lax.all_gather(weight_rows, 'fsdp', axis=0, tiled=True)]
    all_to_all x0 -> x1, starting transfers between devices: none -> 9.71 us  [swapped_in(): pieces = lax.all_to_all(pieces, name, split_axis=0, concat_axis=0)]
  transfers between devices with their start and end apart: 5 -> 5, of which waited for: 5 -> 4; matrix products, arithmetic and copies ran while one was open for 3% -> 5% of each run, Pallas kernels for 0% -> 0%
where the time goes in v1:
time: 764 us; the launch traced here: 763 us
  waiting for transfers between devices  550 us (72%)
  blocking collectives  133 us (17%)
  matrix products  22 us (3%)
  starting transfers between devices  19.9 us (3%)
  between operations  17.1 us (2%)
  local copies, waits for them, and re-layouts  11 us (1%)
  other arithmetic  9.69 us (1%)
    psum x1, waiting for transfers between devices, body(): gain_grad = lax.psum(gain_part, 'fsdp')  231 us
    psum x1, waiting for transfers between devices, body(): total_wv, total_gain = lax.psum((new_wv, new_gain), 'island')  157 us
    all_to_all x1, waiting for transfers between devices, swapped_in(): pieces = lax.all_to_all(pieces, name, split_axis=0, concat_axis=0)  101 us
    psum x1, blocking collectives, body(): total_wv, total_gain = lax.psum((new_wv, new_gain), 'island')  78.1 us
    all_to_all x1, waiting for transfers between devices, body(): lax.all_to_all(normed, 'fsdp', split_axis=1, concat_axis=0, tiled=True)  59.7 us
    psum x1, blocking collectives, body(): weight_square = lax.psum(wv_square, 'fsdp')  55.4 us
  transfers between devices with their start and end apart: 5, of which 4 were waited for; matrix products, arithmetic and copies ran while one was open for 5% of the time, Pallas kernels for 0%

profile of v1, /device:TPU:32, one launch (start us, length us, event | category | flops | bytes accessed | tf_op | source)
XLA Modules:
  0.0 762.8 jit_solution(4802255863670906482)
XLA Ops:
  8.0 0.0 all-gather.3.cloned.1.call-start
  8.1 0.7 all-gather.3.cloned.1.call-update
  8.8 1.9 convert_reduce_fusion
  10.7 2.3 fusion.6
  13.1 2.1 fusion.2
  15.2 4.2 copy.37
  19.3 10.0 %all-to-all-start = ((bf16[128,32,256]{0,2,1:T(8,128)(2,1)}), bf16[128,32,256]{0,2,1:T(8,128)(2,1)}, u32[]{:S(2)}, u32[]{:S(2)}) async-start(bf16[128,32,256]{0,2,1:T(8,128)(2,1)} %bitcast.46), calls=%async_computation | async-start | bytes 4194304 | tf_op jit(solution)/shard_map/all_to_all | solution.py:78
  29.4 1.3 copy.41
  30.7 1.6 copy.40
  32.3 3.5 fusion.38
  35.8 2.1 fusion.13
  37.9 0.1 copy.32
  38.0 59.7 %all-to-all-done = bf16[128,32,256]{0,2,1:T(8,128)(2,1)} async-done(((bf16[128,32,256]{0,2,1:T(8,128)(2,1)}), bf16[128,32,256]{0,2,1:T(8,128)(2,1)}, u32[]{:S(2)}, u32[]{:S(2)}) %all-to-all-start) | async-done | bytes 2097184 | tf_op jit(solution)/shard_map/all_to_all | solution.py:78
  97.7 2.4 stack.2
  100.2 9.7 %all-to-all-start.1 = ((bf16[32,128,512]{2,1,0:T(8,128)(2,1)}), bf16[32,128,512]{2,1,0:T(8,128)(2,1)}, u32[]{:S(2)}, u32[]{:S(2)}) async-start(bf16[32,128,512]{2,1,0:T(8,128)(2,1)} %stack.2), calls=%async_computation.1 | async-start | bytes 8388608 | tf_op jit(solution)/shard_map/all_to_all | solution.py:18
  109.9 0.0 all-reduce.3.cloned.1.call-start
  109.9 0.1 copy.26
  110.1 101.1 %all-to-all-done.1 = bf16[32,128,512]{2,1,0:T(8,128)(2,1)} async-done(((bf16[32,128,512]{2,1,0:T(8,128)(2,1)}), bf16[32,128,512]{2,1,0:T(8,128)(2,1)}, u32[]{:S(2)}, u32[]{:S(2)}) %all-to-all-start.1) | async-done | bytes 4194336 | tf_op jit(solution)/shard_map/all_to_all | solution.py:18
  211.1 5.5 multiply_reduce_fusion.1
  216.6 55.4 %psum.28 = f32[]{:T(128)} all-reduce(f32[]{:T(128)} %get-tuple-element.14), channel_id=1, replica_groups=mesh['island'=16,'fsdp'=32] {'fsdp'}, use_global_device_ids=true, to_apply=%region_5.6 | all-reduce | flops 1 | bytes 8 | tf_op jit(solution)/shard_map/psum | solution.py:98
  272.0 1.2 copy.33
  274.0 0.9 convert_subtract_fusion.1
  274.9 0.0 all-reduce.5.cloned.1.call-start
  275.0 6.6 fusion.1
  281.6 2.3 fusion.29
  283.9 156.8 %all-reduce.3.cloned.1.call-done = f32[256,512]{0,1:T(8,128)} async-done(((f32[256,512]{0,1:T(8,128)}), f32[256,512]{0,1:T(8,128)}) %all-reduce.3.cloned.1.call-update) | async-done | bytes 524304 | tf_op jit(solution)/shard_map/psum | solution.py:108
  440.7 1.4 multiply_subtract_fusion
  442.1 231.4 %all-reduce.5.cloned.1.call-done = f32[16,8192]{1,0:T(8,128)} async-done(((f32[16,8192]{1,0:T(8,128)}), f32[16,8192]{1,0:T(8,128)}) %all-reduce.5.cloned.1.call-update) | async-done | bytes 524304 | tf_op jit(solution)/shard_map/psum | solution.py:90
  673.5 1.8 multiply_reduce_fusion
  676.0 0.7 convert_subtract_fusion.2
  676.7 78.1 %psum.31 = f32[16,256]{1,0:T(8,128)S(1)} all-reduce(f32[16,256]{1,0:T(8,128)S(1)} %convert_subtract_fusion.2), channel_id=1, replica_groups=mesh['island'=16,'fsdp'=32] {'island'}, use_global_device_ids=true, to_apply=%region_9.10 | all-reduce | flops 4096 | bytes 32768 | tf_op jit(solution)/shard_map/psum | solution.py:108
  754.8 0.6 multiply_subtract_fusion.2
  (27 shorter events, 0.2 us)
Async XLA Ops:
  8.0 5.0 copy-start
  8.0 5.0 copy-start.8
  8.0 5.0 copy-start.9
  8.0 267.0 %all-gather.3.cloned.1.call-start = ((), (), s32[]{:S(2)}) async-start(), calls=%async_computation.4 | async-start | bytes 8650752 | tf_op jit(solution)/shard_map/all_gather | solution.py:82
  15.2 14.2 %copy-start.1 = (bf16[128,4096]{1,0:T(8,128)(2,1)S(1)}, bf16[128,4096]{1,0:T(8,128)(2,1)}, u32[]{:S(2)}) copy-start(bf16[128,4096]{1,0:T(8,128)(2,1)} %param.13) | copy-start | bytes 3145732
  19.3 11.3 %copy-start.3 = (bf16[128,512]{1,0:T(8,128)(2,1)S(1)}, bf16[128,512]{1,0:T(8,128)(2,1)}, u32[]{:S(2)}) copy-start(bf16[128,512]{1,0:T(8,128)(2,1)} %param.14) | copy-start | bytes 393220
  19.3 78.4 %all-to-all-start = ((bf16[128,32,256]{0,2,1:T(8,128)(2,1)}), bf16[128,32,256]{0,2,1:T(8,128)(2,1)}, u32[]{:S(2)}, u32[]{:S(2)}) async-start(bf16[128,32,256]{0,2,1:T(8,128)(2,1)} %bitcast.46), calls=%async_computation | async-start | bytes 4194304 | tf_op jit(solution)/shard_map/all_to_all | solution.py:78
  100.2 9.8 %copy-start.2 = (bf16[1,256,512]{2,1,0:T(8,128)(2,1)S(1)}, bf16[1,256,512]{2,1,0:T(8,128)(2,1)}, u32[]{:S(2)}) copy-start(bf16[1,256,512]{2,1,0:T(8,128)(2,1)} %param.16) | copy-start | bytes 786436
  100.2 111.0 %all-to-all-start.1 = ((bf16[32,128,512]{2,1,0:T(8,128)(2,1)}), bf16[32,128,512]{2,1,0:T(8,128)(2,1)}, u32[]{:S(2)}, u32[]{:S(2)}) async-start(bf16[32,128,512]{2,1,0:T(8,128)(2,1)} %stack.2), calls=%async_computation.1 | async-start | bytes 8388608 | tf_op jit(solution)/shard_map/all_to_all | solution.py:18
  109.9 330.8 %all-reduce.3.cloned.1.call-start = ((), (), s32[]{:S(2)}) async-start(), calls=%async_computation.2 | async-start | bytes 1048576 | tf_op jit(solution)/shard_map/psum | solution.py:108
  274.9 398.6 %all-reduce.5.cloned.1.call-start = ((), (), s32[]{:S(2)}) async-start(), calls=%async_computation.3 | async-start | bytes 1048576 | tf_op jit(solution)/shard_map/psum | solution.py:90
  281.6 159.1 %copy-start.4 = (f32[256,32]{0,1:T(8,128)S(1)}, f32[256,32]{0,1:T(8,128)}, u32[]{:S(2)}) copy-start(f32[256,32]{0,1:T(8,128)} %param.18) | copy-start | bytes 98308
  281.6 159.1 %copy-start.5 = (f32[256,32]{0,1:T(8,128)S(1)}, f32[256,32]{0,1:T(8,128)}, u32[]{:S(2)}) copy-start(f32[256,32]{0,1:T(8,128)} %param.19) | copy-start | bytes 98308
  281.6 473.2 %copy-start.6 = (f32[1,256]{1,0:T(1,128)S(1)}, f32[1,256]{1,0:T(1,128)}, u32[]{:S(2)}) copy-start(f32[1,256]{1,0:T(1,128)} %param.20) | copy-start | bytes 3076
  281.6 473.2 %copy-start.7 = (f32[1,256]{1,0:T(1,128)S(1)}, f32[1,256]{1,0:T(1,128)}, u32[]{:S(2)}) copy-start(f32[1,256]{1,0:T(1,128)} %param.21) | copy-start | bytes 3076
Sparse Core Ops, SparseCore 0:
  11.0 138.4 all-gather.2
Sparse Core Ops, SparseCore 1:
  275.0 165.6 all-reduce.2
  443.5 230.0 all-reduce.4
